TPU v7x, 512 devices: a whole 4x4x16 slice. The times are simulated.
512 devices in a mesh: grp: 16 (over z), dev: 32 (over y, x, core).
Axes of the slice: x: 4, y: 4, z: 16, core: 2. Of those that a mesh axis runs over, the one named last changes fastest.
Arguments:
- basis: float32 [2097152, 128], P(('grp', 'dev')), may hold values from -40 to 40
- raw: float32 [2097152, 64], P(('grp', 'dev')), may hold values from -200 to 200, as said below
- recur: float32 [128, 64], replicated, may hold values from -6 to 6
Outputs:
- lanczos: float32 [2097152, 64], P(('grp', 'dev'))
- factor: float32 [64, 64], replicated
- coeffs: float32 [128, 64], replicated
Inputs may be any that keep to these rules, and one draw needn't show every extreme that they name: `raw`: finite real values.
All inputs are finite; a program needn't handle non-finite values.
Results may differ from a plain program's by a relative error of at most 0.0003.
Values sent between devices are 32-bit elements; how exact they have to be, the bound alone decides.
No kernel may reach another device: no remote copies, remote signals or barrier semaphores. Data moves between devices by JAX's collectives and lax.ppermute only.
A program may use at most 64 MiB of HBM per device.

v0:
```python
import jax
import jax.numpy as jnp
from jax import lax
from jax.sharding import Mesh
from jax.sharding import PartitionSpec as P

DEV = ("dev_0", "dev_1", "dev_2")
GRP_DEV = ("grp", "dev_0", "dev_1", "dev_2")


def filled_up(lines, devices):
    spare = -lines.shape[0] % devices
    if not spare:
        return lines
    return jnp.concatenate([lines, jnp.zeros((spare, *lines.shape[1:]), lines.dtype)])


def from_everyone(shard, axis):
    copies = jnp.broadcast_to(shard, (lax.axis_size(axis), *shard.shape))
    return lax.all_to_all(copies, axis, split_axis=0, concat_axis=0, tiled=True)


def laid_out(parts, dim):
    dims = list(parts.shape[1:])
    dims[dim] *= parts.shape[0]
    return jnp.moveaxis(parts, 0, dim).reshape(dims)


def gather_axes(shard, axes, dim):
    far, near = axes
    first = from_everyone(shard, far)
    parts = jnp.swapaxes(from_everyone(first, near), 0, 1)
    return laid_out(parts.reshape(-1, *shard.shape), dim)


def in_blocks(shard, dim, devices):
    before, after = (shard.shape[:dim], shard.shape[dim + 1 :])
    return jnp.moveaxis(shard.reshape(*before, devices, -1, *after), dim, 0)


def sum_at_owner(shard, axis, dim):
    devices = lax.axis_size(axis)
    parts = lax.all_to_all(in_blocks(shard, dim, devices), axis, 0, 0, tiled=True)
    return jnp.sum(parts, axis=0)


def sum_by_axis(shard, axes, dim):
    far, near = axes
    own = sum_at_owner(in_blocks(shard, dim, lax.axis_size(far)), near, dim + 1)
    return jnp.sum(lax.all_to_all(own, far, 0, 0, tiled=True), axis=0)


def nested_sum(shard, axes):
    padded = filled_up(shard, lax.axis_size(axes[0]) * lax.axis_size(axes[1]))
    whole = gather_axes(sum_by_axis(padded, axes, 0), axes, 0)
    return lax.slice_in_dim(whole, 0, len(shard)).reshape(shard.shape)


def packed_total(arrays, axis):
    vector, at, gathered = (jnp.concatenate([a.reshape(-1) for a in arrays]), 0, [])
    running = nested_sum(vector, axis)
    for a in arrays:
        gathered.append(running[at : at + a.size].reshape(a.shape))
        at += a.size
    return tuple(gathered)


def small_factor(moments):
    size = moments.shape[0]
    positions = jnp.arange(size)
    highest = lax.Precision.HIGHEST
    lower_part = jnp.zeros_like(moments)
    for column_index in range(size):
        reduced = moments[:, column_index] - jnp.dot(
            lower_part, lower_part[column_index], precision=highest
        )
        pivot_value = jnp.sqrt(reduced[column_index])
        fresh_column = jnp.where(
            positions > column_index,
            reduced / pivot_value,
            jnp.where(positions == column_index, pivot_value, jnp.zeros_like(reduced)),
        )
        lower_part = jnp.where(
            positions[None, :] == column_index, fresh_column[:, None], lower_part
        )
    return lower_part.T


def small_inverse(upper):
    size = upper.shape[0]
    positions = jnp.arange(size)
    highest = lax.Precision.HIGHEST
    result = jnp.zeros_like(upper)
    for count in range(size):
        row_index = size - 1 - count
        current = upper[row_index]
        target = (positions == row_index).astype(upper.dtype)
        fresh_row = (target - jnp.dot(current, result, precision=highest)) / current[row_index]
        result = jnp.where(positions[:, None] == row_index, fresh_row[None, :], result)
    return result


def factor_pair(moments):
    size = moments.shape[0]
    if size <= 8:
        upper = small_factor(moments)
        return (upper, small_inverse(upper))
    highest = lax.Precision.HIGHEST
    half = size // 2
    upper_one, inverse_one = factor_pair(moments[:half, :half])
    corner = jnp.dot(inverse_one.T, moments[:half, half:], precision=highest)
    rest = moments[half:, half:] - jnp.dot(corner.T, corner, precision=highest)
    upper_two, inverse_two = factor_pair(rest)
    zeros_block = jnp.zeros((size - half, half), moments.dtype)
    upper = jnp.block([[upper_one, corner], [zeros_block, upper_two]])
    inverse_corner = -jnp.dot(
        inverse_one, jnp.dot(corner, inverse_two, precision=highest), precision=highest
    )
    inverse = jnp.block([[inverse_one, inverse_corner], [zeros_block, inverse_two]])
    return (upper, inverse)


def shards(basis, raw, recur):
    highest = lax.Precision.HIGHEST
    total = basis.shape[0] * lax.axis_size("grp") * lax.axis_size(DEV)
    block = raw - jnp.dot(basis, recur, precision=highest)
    cross, basis_gram, block_gram = packed_total(
        (
            jnp.dot(basis.T, block, precision=highest) / total,
            jnp.dot(basis.T, basis, precision=highest) / total,
            jnp.dot(block.T, block, precision=highest) / total,
        ),
        (("grp", "dev_0"), ("dev_1", "dev_2")),
    )
    second = cross - jnp.dot(basis_gram, cross, precision=highest)
    coeffs = cross + second
    twice = block - jnp.dot(basis, coeffs, precision=highest)
    mixed = jnp.dot(cross.T, coeffs, precision=highest)
    gram = (
        block_gram
        - mixed
        - mixed.T
        + jnp.dot(coeffs.T, jnp.dot(basis_gram, coeffs, precision=highest), precision=highest)
    )
    gram = 0.5 * (gram + gram.T)
    factor, inverse = factor_pair(gram)
    lanczos = jnp.dot(twice, inverse, precision=highest)
    return (lanczos, factor, coeffs)


def solution(mesh):
    torus = Mesh(
        mesh.devices.reshape(mesh.shape["grp"], 4, 4, 2), ("grp", "dev_0", "dev_1", "dev_2")
    )
    in_specs = (P(GRP_DEV, None), P(GRP_DEV, None), P())
    out_specs = (P(GRP_DEV, None), P(), P())
    return jax.shard_map(
        shards, mesh=torus, in_specs=in_specs, out_specs=out_specs, check_vma=False
    )
```

profile of v0, /device:TPU:1, one launch (start us, length us, event | category | flops | bytes accessed | tf_op | source)
XLA Modules:
  0.0 258.7 jit_solution(4288992803020659534)
XLA Ops:
  0.7 1.6 copy-done
  2.2 3.5 %fusion.1 = f32[16384]{0:T(1024)S(1)} fusion(f32[4096,128]{1,0:T(8,128)S(1)} %copy-done), kind=kOutput, calls=%fused_computation.4 | convolution fusion | flops 805322752 | bytes 2162688 | tf_op jit(solution)/shard_map/dot_general | solution.py:130
  5.7 2.4 convolution_subtract_fusion
  8.1 1.0 convolution_multiply_fusion.1
  9.1 1.4 fusion.3
  11.8 1.8 reshape.675
  13.6 10.1 %all-to-all-start = ((f32[8,1,3584]{2,1,0:T(1,128)}), f32[8,1,3584]{2,1,0:T(1,128)S(1)}, u32[]{:S(2)}, u32[]{:S(2)}) async-start(f32[8,1,3584]{2,1,0:T(1,128)} %reshape.675), calls=%async_computation | async-start | bytes 229376 | tf_op jit(solution)/shard_map/all_to_all | solution.py:43
  23.7 5.1 %all-to-all-done = f32[8,1,3584]{2,1,0:T(1,128)S(1)} async-done(((f32[8,1,3584]{2,1,0:T(1,128)}), f32[8,1,3584]{2,1,0:T(1,128)S(1)}, u32[]{:S(2)}, u32[]{:S(2)}) %all-to-all-start) | async-done | bytes 114720 | tf_op jit(solution)/shard_map/all_to_all | solution.py:43
  29.4 0.9 reduce.1
  31.1 14.1 %all-to-all-start.1 = ((f32[64,1,56]{2,1,0:T(1,128)}), f32[64,1,56]{2,1,0:T(1,128)S(1)}, u32[]{:S(2)}, u32[]{:S(2)}) async-start(f32[64,1,56]{2,1,0:T(1,128)} %copy.27), calls=%async_computation.1 | async-start | bytes 65536 | tf_op jit(solution)/shard_map/all_to_all | solution.py:50
  45.2 13.4 %all-to-all-done.1 = f32[64,1,56]{2,1,0:T(1,128)S(1)} async-done(((f32[64,1,56]{2,1,0:T(1,128)}), f32[64,1,56]{2,1,0:T(1,128)S(1)}, u32[]{:S(2)}, u32[]{:S(2)}) %all-to-all-start.1) | async-done | bytes 14368 | tf_op jit(solution)/shard_map/all_to_all | solution.py:50
  59.3 4.6 %all-to-all-start.2 = ((f32[64,1,56]{2,1,0:T(1,128)}), f32[64,1,56]{2,1,0:T(1,128)S(1)}, u32[]{:S(2)}, u32[]{:S(2)}) async-start(f32[64,1,56]{2,1,0:T(1,128)} %broadcast_in_dim.1844), calls=%async_computation.2 | async-start | bytes 65536 | tf_op jit(solution)/shard_map/all_to_all | solution.py:20
  63.9 13.5 %all-to-all-done.2 = f32[64,1,56]{2,1,0:T(1,128)S(1)} async-done(((f32[64,1,56]{2,1,0:T(1,128)}), f32[64,1,56]{2,1,0:T(1,128)S(1)}, u32[]{:S(2)}, u32[]{:S(2)}) %all-to-all-start.2) | async-done | bytes 14368 | tf_op jit(solution)/shard_map/all_to_all | solution.py:20
  78.3 6.7 %all-to-all-start.3 = ((f32[8,1,3584]{2,1,0:T(1,128)}), f32[8,1,3584]{2,1,0:T(1,128)S(1)}, u32[]{:S(2)}, u32[]{:S(2)}) async-start(f32[8,1,3584]{2,1,0:T(1,128)} %reshape.677), calls=%async_computation.3 | async-start | bytes 229376 | tf_op jit(solution)/shard_map/all_to_all | solution.py:20
  85.0 5.1 %all-to-all-done.3 = f32[8,1,3584]{2,1,0:T(1,128)S(1)} async-done(((f32[8,1,3584]{2,1,0:T(1,128)}), f32[8,1,3584]{2,1,0:T(1,128)S(1)}, u32[]{:S(2)}, u32[]{:S(2)}) %all-to-all-start.3) | async-done | bytes 114720 | tf_op jit(solution)/shard_map/all_to_all | solution.py:20
  90.2 1.6 reduce.2
  91.7 1.0 reshape.678
  93.4 1.1 copy.29
  96.5 1.1 fusion.2
  97.7 1.1 fusion.1414
  99.1 3.3 %fusion = f32[4096,64]{0,1:T(8,128)} fusion(f32[4096,64]{0,1:T(8,128)S(1)} %convolution_subtract_fusion, f32[128,64]{0,1:T(8,128)S(1)} %fusion.2, f32[4096,128]{1,0:T(8,128)S(1)} %copy-done), kind=kOutput, calls=%fused_computation.2 | convolution fusion | flops 402915328 | bytes 4227072 | tf_op jit(solution)/shard_map/dot_general | solution.py:137
  117.0 0.9 fusion.18
  135.8 0.9 fusion.41
  256.7 2.1 fusion.193
  (405 shorter events, 119.3 us)
Async XLA Ops:
  0.6 1.6 copy-start
  0.6 5.0 %copy-start.4 = (f32[128,64]{0,1:T(8,128)S(1)}, f32[128,64]{0,1:T(8,128)}, u32[]{:S(2)}) copy-start(f32[128,64]{0,1:T(8,128)} %param.5) | copy-start | bytes 98308
  2.2 3.5 %copy-start.2 = (f32[4096,64]{0,1:T(8,128)S(1)}, f32[4096,64]{0,1:T(8,128)}, u32[]{:S(2)}) copy-start(f32[4096,64]{0,1:T(8,128)} %param.4) | copy-start | bytes 3145732
  13.6 15.3 %all-to-all-start = ((f32[8,1,3584]{2,1,0:T(1,128)}), f32[8,1,3584]{2,1,0:T(1,128)S(1)}, u32[]{:S(2)}, u32[]{:S(2)}) async-start(f32[8,1,3584]{2,1,0:T(1,128)} %reshape.675), calls=%async_computation | async-start | bytes 229376 | tf_op jit(solution)/shard_map/all_to_all | solution.py:43
  31.1 27.5 %all-to-all-start.1 = ((f32[64,1,56]{2,1,0:T(1,128)}), f32[64,1,56]{2,1,0:T(1,128)S(1)}, u32[]{:S(2)}, u32[]{:S(2)}) async-start(f32[64,1,56]{2,1,0:T(1,128)} %copy.27), calls=%async_computation.1 | async-start | bytes 65536 | tf_op jit(solution)/shard_map/all_to_all | solution.py:50
  59.3 18.1 %all-to-all-start.2 = ((f32[64,1,56]{2,1,0:T(1,128)}), f32[64,1,56]{2,1,0:T(1,128)S(1)}, u32[]{:S(2)}, u32[]{:S(2)}) async-start(f32[64,1,56]{2,1,0:T(1,128)} %broadcast_in_dim.1844), calls=%async_computation.2 | async-start | bytes 65536 | tf_op jit(solution)/shard_map/all_to_all | solution.py:20
  78.3 11.9 %all-to-all-start.3 = ((f32[8,1,3584]{2,1,0:T(1,128)}), f32[8,1,3584]{2,1,0:T(1,128)S(1)}, u32[]{:S(2)}, u32[]{:S(2)}) async-start(f32[8,1,3584]{2,1,0:T(1,128)} %reshape.677), calls=%async_computation.3 | async-start | bytes 229376 | tf_op jit(solution)/shard_map/all_to_all | solution.py:20
  97.7 4.9 %copy-start.3 = (f32[128,64]{0,1:T(8,128)}, f32[128,64]{0,1:T(8,128)S(1)}, u32[]{:S(2)}) copy-start(f32[128,64]{0,1:T(8,128)S(1)} %fusion.2) | copy-start | bytes 98308
  99.0 3.4 %slice-start = ((f32[448,64]{1,0:T(8,128)}), f32[64,64]{1,0:T(8,128)S(1)}, s32[]{:S(2)}) async-start(f32[448,64]{1,0:T(8,128)} %slice.1170), calls=%async_computation.4 | async-start | bytes 65536 | tf_op jit(solution)/shard_map/slice | solution.py:63
  233.2 23.4 %copy-start.1 = (f32[4096,64]{0,1:T(8,128)S(1)}, f32[4096,64]{0,1:T(8,128)}, u32[]{:S(2)}) copy-start(f32[4096,64]{0,1:T(8,128)} %fusion) | copy-start | bytes 3145732
where the time goes:
time: 260 us; the launch traced here: 259 us
  matrix products  83.6 us (32%)
  local copies, waits for them, and re-layouts  51.4 us (20%)
  between operations  41.2 us (16%)
  waiting for transfers between devices  37.1 us (14%)
  starting transfers between devices  35.6 us (14%)
  other arithmetic  9.86 us (4%)
    dot_general x64, matrix products, small_inverse(): jnp.dot(current, result, precision=highest)  52.6 us
    slice x56, local copies, waits for them, and re-layouts, small_factor(): pivot_value = jnp.sqrt(reduced[column_index])  33.2 us
    all_to_all x2, waiting for transfers between devices, from_everyone(): return lax.all_to_all(copies, axis, split_axis=0, concat_axis=0, tiled=True)  18.6 us
    all_to_all x1, starting transfers between devices, sum_by_axis(): return jnp.sum(lax.all_to_all(own, far, 0, 0, tiled=True), axis=0)  14.1 us
    all_to_all x1, waiting for transfers between devices, sum_by_axis(): return jnp.sum(lax.all_to_all(own, far, 0, 0, tiled=True), axis=0)  13.4 us
    all_to_all x2, starting transfers between devices, from_everyone(): return lax.all_to_all(copies, axis, split_axis=0, concat_axis=0, tiled=True)  11.3 us
    all_to_all x1, starting transfers between devices, sum_at_owner(): lax.all_to_all(in_blocks(shard, dim, devices), axis, 0, 0, tiled=True)  10.1 us
    dot_general x57, matrix products, small_factor(): jnp.dot(lower_part, lower_part[column_index], precision=highest)  9.62 us
  transfers between devices with their start and end apart: 4, of which 4 were waited for; matrix products, arithmetic and copies ran while one was open for 0% of the time, Pallas kernels for 0%

commit v1 on v0

--- a/solution.py
+++ b/solution.py
@@ -3,6 +3,8 @@
 from jax import lax
 from jax.sharding import Mesh
 from jax.sharding import PartitionSpec as P
+from jax.experimental import pallas as pl
+from jax.experimental.pallas import tpu as pltpu
 
 DEV = ("dev_0", "dev_1", "dev_2")
 GRP_DEV = ("grp", "dev_0", "dev_1", "dev_2")
@@ -120,6 +122,44 @@
     return (upper, inverse)
 
 
+def eliminate(augmented_ref, factor_ref, inverse_t_ref):
+    matrix = augmented_ref[...]
+    size = matrix.shape[0]
+    rows = lax.broadcasted_iota(jnp.int32, matrix.shape, 0)
+    lanes = lax.broadcasted_iota(jnp.int32, matrix.shape, 1)
+    row_ids = rows[:, :1]
+
+    def step(index, matrix):
+        pivot_row = jnp.sum(jnp.where(rows == index, matrix, 0.0), axis=0, keepdims=True)
+        column = jnp.sum(jnp.where(lanes == index, matrix, 0.0), axis=1, keepdims=True)
+        pivot = jnp.sum(jnp.where(lanes[:1] == index, pivot_row, 0.0), axis=1, keepdims=True)
+        scale = jnp.where(row_ids > index, column / pivot, 0.0)
+        return matrix - scale * pivot_row
+
+    matrix = lax.fori_loop(0, size, step, matrix)
+    diagonal = jnp.sum(jnp.where(lanes == rows, matrix, 0.0), axis=1, keepdims=True)
+    root = jnp.sqrt(diagonal)
+    scaled = matrix / root
+    upper = jnp.where(lanes > rows, scaled, jnp.where(lanes == rows, root, 0.0))
+    factor_ref[...] = upper[:, :size]
+    inverse_t_ref[...] = scaled[:, size:]
+
+
+def factor_and_inverse_t(gram):
+    size = gram.shape[0]
+    augmented = jnp.concatenate([gram, jnp.eye(size, dtype=gram.dtype)], axis=1)
+    vmem = pl.BlockSpec(memory_space=pltpu.VMEM)
+    return pl.pallas_call(
+        eliminate,
+        out_shape=(
+            jax.ShapeDtypeStruct((size, size), gram.dtype),
+            jax.ShapeDtypeStruct((size, size), gram.dtype),
+        ),
+        in_specs=[vmem],
+        out_specs=(vmem, vmem),
+    )(augmented)
+
+
 def shards(basis, raw, recur):
     highest = lax.Precision.HIGHEST
     total = basis.shape[0] * lax.axis_size("grp") * lax.axis_size(DEV)
@@ -143,8 +183,8 @@
         + jnp.dot(coeffs.T, jnp.dot(basis_gram, coeffs, precision=highest), precision=highest)
     )
     gram = 0.5 * (gram + gram.T)
-    factor, inverse = factor_pair(gram)
-    lanczos = jnp.dot(twice, inverse, precision=highest)
+    factor, inverse_t = factor_and_inverse_t(gram)
+    lanczos = lax.dot_general(twice, inverse_t, (((1,), (1,)), ((), ())), precision=highest)
     return (lanczos, factor, coeffs)
 
 

time: 260 us -> 111 us (0.43)
  matrix products: 83.6 us -> 17.5 us
  blocking collectives: 0 us -> 59.8 us
  local copies, waits for them, and re-layouts: 51.4 us -> 9.69 us
  between operations: 41.2 us -> 0.83 us
  waiting for transfers between devices: 37.1 us -> 5.13 us
  starting transfers between devices: 35.6 us -> 6.73 us
  Pallas kernels: 0 us -> 8.13 us
  other arithmetic: 9.86 us -> 2.65 us
    dot_general x150 -> x1, matrix products: 69.3 us -> 3.27 us  [shards(): lax.dot_general(twice, inverse_t, (((1,), (1,)), ((), ())), precision=hig...]
    all_to_all x0 -> x3, blocking collectives: none -> 59.8 us  [the longest x1 28 us: sum_by_axis(): return jnp.sum(lax.all_to_all(own, far, 0, 0, tiled=True), axis=0)]
    slice x64 -> x0, local copies, waits for them, and re-layouts: 38.7 us -> none  [the longest x56 33.2 us: small_factor(): pivot_value = jnp.sqrt(reduced[column_index])]
    all_to_all x2 -> x0, starting transfers between devices: 24.2 us -> none  [the longest x1 14.1 us: sum_by_axis(): return jnp.sum(lax.all_to_all(own, far, 0, 0, tiled=True), axis=0)]
    all_to_all x2 -> x0, waiting for transfers between devices: 18.5 us -> none  [the longest x1 13.4 us: sum_by_axis(): return jnp.sum(lax.all_to_all(own, far, 0, 0, tiled=True), axis=0)]
    all_to_all x2 -> x1, waiting for transfers between devices: 18.6 us -> 5.13 us  [from_everyone(): return lax.all_to_all(copies, axis, split_axis=0, concat_axis=0, tiled=True)]
    pallas_call x0 -> x1, Pallas kernels: none -> 8.13 us  [factor_and_inverse_t(): pl.pallas_call(eliminate, out_shape=(jax.ShapeDtypeStruct((size, size), g...]
    select_n x136 -> x0, other arithmetic: 5.97 us -> none  [the longest x64 4.92 us: small_factor(): jnp.where(positions[None, :] == column_index, fresh_column[:, None], lowe...]
  transfers between devices with their start and end apart: 4 -> 1, of which waited for: 4 -> 1; matrix products, arithmetic and copies ran while one was open for 0% -> 0% of each run, Pallas kernels for 0% -> 0%
where the time goes in v1:
time: 111 us; the launch traced here: 110 us
  blocking collectives  59.8 us (54%)
  matrix products  17.5 us (16%)
  local copies, waits for them, and re-layouts  9.69 us (9%)
  Pallas kernels  8.13 us (7%)
  starting transfers between devices  6.73 us (6%)
  waiting for transfers between devices  5.13 us (5%)
  other arithmetic  2.65 us (2%)
    all_to_all x1, blocking collectives, sum_by_axis(): return jnp.sum(lax.all_to_all(own, far, 0, 0, tiled=True), axis=0)  28 us
    all_to_all x1, blocking collectives, from_everyone(): return lax.all_to_all(copies, axis, split_axis=0, concat_axis=0, tiled=True)  17.4 us
    all_to_all x1, blocking collectives, sum_at_owner(): lax.all_to_all(in_blocks(shard, dim, devices), axis, 0, 0, tiled=True)  14.4 us
    pallas_call x1, Pallas kernels, factor_and_inverse_t(): pl.pallas_call(eliminate, out_shape=(jax.ShapeDtypeStruct((size, size), g...  8.13 us
    all_to_all x1, starting transfers between devices, from_everyone(): return lax.all_to_all(copies, axis, split_axis=0, concat_axis=0, tiled=True)  6.73 us
    all_to_all x1, waiting for transfers between devices, from_everyone(): return lax.all_to_all(copies, axis, split_axis=0, concat_axis=0, tiled=True)  5.13 us
    unnamed x16, local copies, waits for them, and re-layouts  4.72 us
    dot_general x1, matrix products, shards(): jnp.dot(basis.T, basis, precision=highest) / total  3.45 us
  transfers between devices with their start and end apart: 1, of which 1 were waited for; matrix products, arithmetic and copies ran while one was open for 0% of the time, Pallas kernels for 0%

profile of v1, /device:TPU:1, one launch (start us, length us, event | category | flops | bytes accessed | tf_op | source)
XLA Modules:
  0.0 110.5 jit_solution(394472355023447930)
XLA Ops:
  0.7 1.6 %copy-done = f32[4096,128]{1,0:T(8,128)S(1)} copy-done((f32[4096,128]{1,0:T(8,128)S(1)}, f32[4096,128]{1,0:T(8,128)}, u32[]{:S(2)}) %copy-start) | copy-done | bytes 2097176
  2.2 3.5 %fusion.1 = f32[16384]{0:T(1024)S(1)} fusion(f32[4096,128]{1,0:T(8,128)S(1)} %copy-done), kind=kOutput, calls=%fused_computation.4 | convolution fusion | flops 805322752 | bytes 2162688 | tf_op jit(solution)/shard_map/dot_general | solution.py:170
  5.7 2.4 %convolution_subtract_fusion = f32[4096,64]{0,1:T(8,128)S(1)} fusion(f32[4096,64]{0,1:T(8,128)S(1)} %copy-done.1, f32[4096,128]{1,0:T(8,128)S(1)} %copy-done, f32[128,64]{0,1:T(8,128)S(1)} %copy-done.3), kind=kOutput, calls=%fused_computation | convolution fusion | flops 402915328 | bytes 4227072 | tf_op jit(solution)/shard_map/dot_general | solution.py:166
  8.1 1.0 convolution_multiply_fusion.1
  9.1 1.4 %fusion.3 = f32[128,64]{0,1:T(8,128)S(1)} fusion(f32[4096,64]{0,1:T(8,128)S(1)} %convolution_subtract_fusion, f32[4096,128]{1,0:T(8,128)S(1)} %copy-done), kind=kOutput, calls=%fused_computation.10 | convolution fusion | flops 402661376 | bytes 3178496 | tf_op jit(solution)/shard_map/dot_general | solution.py:169
  11.0 0.8 copy.26
  11.8 1.1 reshape.33
  12.9 14.4 %all_to_all.28 = f32[8,1,3584]{2,1,0:T(1,128)S(1)} all-to-all(f32[8,1,3584]{2,1,0:T(1,128)S(1)} %reshape.33), channel_id=1, replica_groups=mesh['grp'=16,'dev_0'=4,'dev_1'=4,'dev_2'=2] {'dev_1','dev_2'}, dimensions={0} | all-to-all | bytes 229376 | tf_op jit(solution)/shard_map/all_to_all | solution.py:45
  27.8 0.9 reduce.1
  28.9 28.0 %all_to_all.29 = f32[64,1,56]{2,1,0:T(1,128)S(1)} all-to-all(f32[64,1,56]{2,1,0:T(1,128)S(1)} %copy.27), channel_id=1, replica_groups=mesh['grp'=16,'dev_0'=4,'dev_1'=4,'dev_2'=2] {'grp','dev_0'}, dimensions={0} | all-to-all | bytes 28672 | tf_op jit(solution)/shard_map/all_to_all | solution.py:52
  57.1 17.4 %all_to_all.30 = f32[64,1,56]{2,1,0:T(1,128)S(1)} all-to-all(f32[64,1,56]{2,1,0:T(1,128)S(1)} %broadcast_in_dim.6), channel_id=1, replica_groups=mesh['grp'=16,'dev_0'=4,'dev_1'=4,'dev_2'=2] {'grp','dev_0'}, dimensions={0} | all-to-all | bytes 28672 | tf_op jit(solution)/shard_map/all_to_all | solution.py:22
  74.5 0.8 reshape.35
  75.4 6.7 %all-to-all-start.3 = ((f32[8,1,3584]{2,1,0:T(1,128)}), f32[8,1,3584]{2,1,0:T(1,128)S(1)}, u32[]{:S(2)}, u32[]{:S(2)}) async-start(f32[8,1,3584]{2,1,0:T(1,128)} %reshape.35), calls=%async_computation.3 | async-start | bytes 229376 | tf_op jit(solution)/shard_map/all_to_all | solution.py:22
  82.1 5.1 %all-to-all-done.3 = f32[8,1,3584]{2,1,0:T(1,128)S(1)} async-done(((f32[8,1,3584]{2,1,0:T(1,128)}), f32[8,1,3584]{2,1,0:T(1,128)S(1)}, u32[]{:S(2)}, u32[]{:S(2)}) %all-to-all-start.3) | async-done | bytes 114720 | tf_op jit(solution)/shard_map/all_to_all | solution.py:22
  87.2 0.9 reduce.2
  88.3 0.7 bitcast_bitcast_fusion
  89.0 1.1 copy.29
  90.2 0.9 slice.16
  91.1 0.8 slice.21
  92.0 1.1 %fusion.2 = f32[128,64]{0,1:T(8,128)S(1)} fusion(f32[128,64]{0,1:T(8,128)S(1)} %copy.37, f32[224,128]{1,0:T(8,128)S(1)} %slice.18, f32[448,64]{1,0:T(8,128)} %slice.16), kind=kOutput, calls=%fused_computation.7 | convolution fusion | flops 12599296 | bytes 196608 | tf_op jit(solution)/shard_map/dot_general | solution.py:175
  93.2 1.1 %fusion.9 = f32[64,64]{1,0:T(8,128)S(1)} fusion(f32[128,64]{0,1:T(8,128)S(1)} %fusion.2, f32[448,64]{1,0:T(8,128)} %slice.16), kind=kOutput, calls=%fused_computation.21 | convolution fusion | flops 6291456 | bytes 114688 | tf_op jit(solution)/shard_map/dot_general | solution.py:178
  94.6 3.4 %fusion = f32[4096,64]{0,1:T(8,128)} fusion(f32[4096,64]{0,1:T(8,128)S(1)} %convolution_subtract_fusion, f32[128,64]{0,1:T(8,128)S(1)} %fusion.2, f32[4096,128]{1,0:T(8,128)S(1)} %copy-done), kind=kOutput, calls=%fused_computation.2 | convolution fusion | flops 402915328 | bytes 4227072 | tf_op jit(solution)/shard_map/dot_general | solution.py:177
  99.1 8.1 %shard_map.58 = (f32[64,64]{1,0:T(8,128)}, f32[64,64]{1,0:T(8,128)}) custom-call(f32[64,128]{1,0:T(8,128)} %pad_maximum_fusion.1.augmented_ref), custom_call_target="tpu_custom_call" | custom-call | tf_op jit(solution)/shard_map/pallas_call | solution.py:152
  107.2 3.3 %fusion.12 = f32[4096,64]{0,1:T(8,128)} fusion(f32[4096,64]{0,1:T(8,128)} %fusion, f32[64,64]{1,0:T(8,128)} %get-tuple-element.5), kind=kOutput, calls=%fused_computation.27 | convolution fusion | flops 201326592 | bytes 2113536 | tf_op jit(solution)/shard_map/dot_general | solution.py:187
  (33 shorter events, 3.1 us)
Async XLA Ops:
  0.6 1.6 %copy-start = (f32[4096,128]{1,0:T(8,128)S(1)}, f32[4096,128]{1,0:T(8,128)}, u32[]{:S(2)}) copy-start(f32[4096,128]{1,0:T(8,128)} %param.3) | copy-start | bytes 6291460
  0.6 5.0 %copy-start.3 = (f32[128,64]{0,1:T(8,128)S(1)}, f32[128,64]{0,1:T(8,128)}, u32[]{:S(2)}) copy-start(f32[128,64]{0,1:T(8,128)} %param.5) | copy-start | bytes 98308
  2.2 3.5 %copy-start.1 = (f32[4096,64]{0,1:T(8,128)S(1)}, f32[4096,64]{0,1:T(8,128)}, u32[]{:S(2)}) copy-start(f32[4096,64]{0,1:T(8,128)} %param.4) | copy-start | bytes 3145732
  75.4 11.9 %all-to-all-start.3 = ((f32[8,1,3584]{2,1,0:T(1,128)}), f32[8,1,3584]{2,1,0:T(1,128)S(1)}, u32[]{:S(2)}, u32[]{:S(2)}) async-start(f32[8,1,3584]{2,1,0:T(1,128)} %reshape.35), calls=%async_computation.3 | async-start | bytes 229376 | tf_op jit(solution)/shard_map/all_to_all | solution.py:22
  93.2 4.9 %copy-start.2 = (f32[128,64]{0,1:T(8,128)}, f32[128,64]{0,1:T(8,128)S(1)}, u32[]{:S(2)}) copy-start(f32[128,64]{0,1:T(8,128)S(1)} %fusion.2) | copy-start | bytes 98308
  94.6 3.4 %slice-start = ((f32[448,64]{1,0:T(8,128)}), f32[64,64]{1,0:T(8,128)S(1)}, s32[]{:S(2)}) async-start(f32[448,64]{1,0:T(8,128)} %slice.16), calls=%async_computation.4 | async-start | bytes 65536 | tf_op jit(solution)/shard_map/slice | solution.py:65

commit v2 on v1

--- a/solution.py
+++ b/solution.py
@@ -60,7 +60,7 @@
 
 def packed_total(arrays, axis):
     vector, at, gathered = (jnp.concatenate([a.reshape(-1) for a in arrays]), 0, [])
-    running = nested_sum(vector, axis)
+    running = lax.psum(vector, axis)
     for a in arrays:
         gathered.append(running[at : at + a.size].reshape(a.shape))
         at += a.size
@@ -170,7 +170,7 @@
             jnp.dot(basis.T, basis, precision=highest) / total,
             jnp.dot(block.T, block, precision=highest) / total,
         ),
-        (("grp", "dev_0"), ("dev_1", "dev_2")),
+        GRP_DEV,
     )
     second = cross - jnp.dot(basis_gram, cross, precision=highest)
     coeffs = cross + second

time: 111 us -> 494 us (4.45)
  waiting for transfers between devices: 5.13 us -> 450 us
  blocking collectives: 59.8 us -> 0 us
  between operations: 0.83 us -> 14.2 us
  starting transfers between devices: 6.73 us -> 0.04 us
  local copies, waits for them, and re-layouts: 9.69 us -> 3 us
    psum x0 -> x1, waiting for transfers between devices: none -> 450 us  [packed_total(): running = lax.psum(vector, axis)]
    all_to_all x3 -> x0, blocking collectives: 59.8 us -> none  [the longest x1 28 us: sum_by_axis(): return jnp.sum(lax.all_to_all(own, far, 0, 0, tiled=True), axis=0)]
    all_to_all x1 -> x0, starting transfers between devices: 6.73 us -> none  [from_everyone(): return lax.all_to_all(copies, axis, split_axis=0, concat_axis=0, tiled=True)]
    all_to_all x1 -> x0, waiting for transfers between devices: 5.13 us -> none  [from_everyone(): return lax.all_to_all(copies, axis, split_axis=0, concat_axis=0, tiled=True)]
where the time goes in v2:
time: 494 us
  waiting for transfers between devices  450 us (91%)
  matrix products  16.7 us (3%)
  between operations  14.2 us (3%)
  Pallas kernels  8.14 us (2%)
    psum x1, waiting for transfers between devices, packed_total(): running = lax.psum(vector, axis)  450 us
  transfers between devices with their start and end apart: 1, of which 1 were waited for; matrix products, arithmetic and copies ran while one was open for 0% of the time, Pallas kernels for 0%

profile of v2, /device:TPU:1, one launch (start us, length us, event | category | flops | bytes accessed | tf_op | source)
XLA Modules:
  0.0 493.7 jit_solution(16827534911016020026)
XLA Ops:
  7.2 1.5 copy-done
  8.8 3.5 fusion.1
  12.2 2.4 convolution_subtract_fusion
  14.7 1.0 convolution_multiply_fusion.1
  15.6 1.4 fusion.3
  17.0 0.1 reshape.48
  17.1 0.1 copy.9
  17.2 0.1 reshape.46
  17.3 0.7 pad_maximum_fusion
  18.0 450.2 %all-reduce.2.cloned.1.call-done = f32[28672]{0:T(1024)} async-done(((f32[28672]{0:T(1024)}), f32[28672]{0:T(1024)}) %all-reduce.2.cloned.1.call-update) | async-done | bytes 114704 | tf_op jit(solution)/shard_map/psum | solution.py:63
  468.2 0.8 slice.39
  468.9 0.1 reshape.49
  469.1 1.1 fusion.2
  470.2 0.3 fusion.7
  470.5 3.3 fusion
  473.9 0.1 reshape.50
  473.9 0.1 copy.12
  474.0 0.1 copy.13
  474.1 0.2 fusion.4
  474.3 0.3 convolution_add_fusion
  474.6 0.1 copy.15
  474.7 0.7 pad_maximum_fusion.1.augmented_ref
  475.4 8.1 %shard_map.58 = (f32[64,64]{1,0:T(8,128)}, f32[64,64]{1,0:T(8,128)}) custom-call(f32[64,128]{1,0:T(8,128)} %pad_maximum_fusion.1.augmented_ref), custom_call_target="tpu_custom_call" | custom-call | tf_op jit(solution)/shard_map/pallas_call | solution.py:152
  483.6 3.3 fusion.8
  (16 shorter events, 0.2 us)
Async XLA Ops:
  7.2 1.6 copy-start
  7.2 5.0 %copy-start.4 = (f32[128,64]{0,1:T(8,128)S(1)}, f32[128,64]{0,1:T(8,128)}, u32[]{:S(2)}) copy-start(f32[128,64]{0,1:T(8,128)} %param.5) | copy-start | bytes 98308
  7.2 461.0 %all-reduce.2.cloned.1.call-start = ((), (), s32[]{:S(2)}) async-start(), calls=%async_computation | async-start | bytes 229376 | tf_op jit(solution)/shard_map/psum | solution.py:63
  8.8 3.5 copy-start.1
  470.2 4.1 copy-start.2
  470.5 3.4 slice-start
  470.5 3.6 copy-start.3
Sparse Core Ops, SparseCore 0:
  18.1 450.0 all-reduce.1

commit v3 on v1

--- a/solution.py
+++ b/solution.py
@@ -10,52 +10,31 @@
 GRP_DEV = ("grp", "dev_0", "dev_1", "dev_2")
 
 
-def filled_up(lines, devices):
-    spare = -lines.shape[0] % devices
-    if not spare:
-        return lines
-    return jnp.concatenate([lines, jnp.zeros((spare, *lines.shape[1:]), lines.dtype)])
+def group_size(axes):
+    size = 1
+    for axis in axes:
+        size *= lax.axis_size(axis)
+    return size
 
 
-def from_everyone(shard, axis):
-    copies = jnp.broadcast_to(shard, (lax.axis_size(axis), *shard.shape))
-    return lax.all_to_all(copies, axis, split_axis=0, concat_axis=0, tiled=True)
+def from_everyone(shard, axes):
+    copies = jnp.broadcast_to(shard, (group_size(axes), *shard.shape))
+    return lax.all_to_all(copies, axes, 0, 0, tiled=True)
 
 
-def laid_out(parts, dim):
-    dims = list(parts.shape[1:])
-    dims[dim] *= parts.shape[0]
-    return jnp.moveaxis(parts, 0, dim).reshape(dims)
-
-
-def gather_axes(shard, axes, dim):
-    far, near = axes
-    first = from_everyone(shard, far)
-    parts = jnp.swapaxes(from_everyone(first, near), 0, 1)
-    return laid_out(parts.reshape(-1, *shard.shape), dim)
-
-
-def in_blocks(shard, dim, devices):
-    before, after = (shard.shape[:dim], shard.shape[dim + 1 :])
-    return jnp.moveaxis(shard.reshape(*before, devices, -1, *after), dim, 0)
-
-
-def sum_at_owner(shard, axis, dim):
-    devices = lax.axis_size(axis)
-    parts = lax.all_to_all(in_blocks(shard, dim, devices), axis, 0, 0, tiled=True)
+def scatter_sum(vector, axes):
+    parts = lax.all_to_all(vector.reshape(group_size(axes), -1), axes, 0, 0, tiled=True)
     return jnp.sum(parts, axis=0)
 
 
-def sum_by_axis(shard, axes, dim):
-    far, near = axes
-    own = sum_at_owner(in_blocks(shard, dim, lax.axis_size(far)), near, dim + 1)
-    return jnp.sum(lax.all_to_all(own, far, 0, 0, tiled=True), axis=0)
-
-
-def nested_sum(shard, axes):
-    padded = filled_up(shard, lax.axis_size(axes[0]) * lax.axis_size(axes[1]))
-    whole = gather_axes(sum_by_axis(padded, axes, 0), axes, 0)
-    return lax.slice_in_dim(whole, 0, len(shard)).reshape(shard.shape)
+def nested_sum(vector, axes):
+    near, far = axes
+    devices = group_size(near)
+    padded = jnp.pad(vector, (0, -vector.shape[0] % devices))
+    own = scatter_sum(padded, near)
+    own = jnp.sum(from_everyone(own, far), axis=0)
+    whole = from_everyone(own, near).reshape(-1)
+    return whole[: vector.shape[0]]
 
 
 def packed_total(arrays, axis):
@@ -170,7 +149,7 @@
             jnp.dot(basis.T, basis, precision=highest) / total,
             jnp.dot(block.T, block, precision=highest) / total,
         ),
-        (("grp", "dev_0"), ("dev_1", "dev_2")),
+        (DEV, ("grp",)),
     )
     second = cross - jnp.dot(basis_gram, cross, precision=highest)
     coeffs = cross + second

time: 111 us -> 88.1 us (0.79)
  blocking collectives: 59.8 us -> 42.3 us
  local copies, waits for them, and re-layouts: 9.69 us -> 5.13 us
  waiting for transfers between devices: 5.13 us -> 6.98 us
  starting transfers between devices: 6.73 us -> 5.32 us
    all_to_all x3 -> x2, blocking collectives: 59.8 us -> 42.3 us  [the longest x1 25.2 us: from_everyone(): return lax.all_to_all(copies, axes, 0, 0, tiled=True)]
    transpose x3 -> x0, local copies, waits for them, and re-layouts: 2.63 us -> none  [the longest x2 1.79 us: gather_axes(): parts = jnp.swapaxes(from_everyone(first, near), 0, 1)]
    unnamed x16 -> x15, local copies, waits for them, and re-layouts: 4.72 us -> 2.39 us
    all_to_all x1, waiting for transfers between devices: 5.13 us -> 6.98 us  [from_everyone(): return lax.all_to_all(copies, axes, 0, 0, tiled=True)]
    all_to_all x1, starting transfers between devices: 6.73 us -> 5.32 us  [from_everyone(): return lax.all_to_all(copies, axes, 0, 0, tiled=True)]
  transfers between devices with their start and end apart: 1 -> 1, of which waited for: 1 -> 1; matrix products, arithmetic and copies ran while one was open for 0% -> 1% of each run, Pallas kernels for 0% -> 0%
where the time goes in v3:
time: 88.1 us; the launch traced here: 87.7 us
  blocking collectives  42.3 us (48%)
  matrix products  16.6 us (19%)
  Pallas kernels  8.15 us (9%)
  waiting for transfers between devices  6.98 us (8%)
  starting transfers between devices  5.32 us (6%)
  local copies, waits for them, and re-layouts  5.13 us (6%)
  other arithmetic  2.38 us (3%)
    all_to_all x1, blocking collectives, from_everyone(): return lax.all_to_all(copies, axes, 0, 0, tiled=True)  25.2 us
    all_to_all x1, blocking collectives, scatter_sum(): lax.all_to_all(vector.reshape(group_size(axes), -1), axes, 0, 0, tiled=True)  17.1 us
    pallas_call x1, Pallas kernels, factor_and_inverse_t(): pl.pallas_call(eliminate, out_shape=(jax.ShapeDtypeStruct((size, size), g...  8.15 us
    all_to_all x1, waiting for transfers between devices, from_everyone(): return lax.all_to_all(copies, axes, 0, 0, tiled=True)  6.98 us
    all_to_all x1, starting transfers between devices, from_everyone(): return lax.all_to_all(copies, axes, 0, 0, tiled=True)  5.32 us
    dot_general x1, matrix products, shards(): jnp.dot(basis.T, basis, precision=highest) / total  3.45 us
    dot_general x1, matrix products, shards(): twice = block - jnp.dot(basis, coeffs, precision=highest)  3.36 us
    dot_general x1, matrix products, shards(): lax.dot_general(twice, inverse_t, (((1,), (1,)), ((), ())), precision=hig...  3.27 us
  transfers between devices with their start and end apart: 1, of which 1 were waited for; matrix products, arithmetic and copies ran while one was open for 1% of the time, Pallas kernels for 0%

profile of v3, /device:TPU:1, one launch (start us, length us, event | category | flops | bytes accessed | tf_op | source)
XLA Modules:
  0.0 87.7 jit_solution(1656865782728988907)
XLA Ops:
  0.7 1.6 %copy-done = f32[4096,128]{1,0:T(8,128)S(1)} copy-done((f32[4096,128]{1,0:T(8,128)S(1)}, f32[4096,128]{1,0:T(8,128)}, u32[]{:S(2)}) %copy-start) | copy-done | bytes 2097176
  2.2 3.5 %fusion.1 = f32[16384]{0:T(1024)S(1)} fusion(f32[4096,128]{1,0:T(8,128)S(1)} %copy-done), kind=kOutput, calls=%fused_computation.4 | convolution fusion | flops 805322752 | bytes 2162688 | tf_op jit(solution)/shard_map/dot_general | solution.py:149
  5.7 2.4 %convolution_subtract_fusion = f32[4096,64]{0,1:T(8,128)S(1)} fusion(f32[4096,64]{0,1:T(8,128)S(1)} %copy-done.1, f32[4096,128]{1,0:T(8,128)S(1)} %copy-done, f32[128,64]{0,1:T(8,128)S(1)} %copy-done.5), kind=kOutput, calls=%fused_computation | convolution fusion | flops 402915328 | bytes 4227072 | tf_op jit(solution)/shard_map/dot_general | solution.py:145
  8.1 1.0 %convolution_multiply_fusion.1 = f32[64,64]{1,0:T(8,128)S(1)} fusion(f32[4096,64]{0,1:T(8,128)S(1)} %convolution_subtract_fusion), kind=kOutput, calls=%fused_computation.8 | convolution fusion | flops 201330688 | bytes 1064960 | tf_op jit(solution)/shard_map/dot_general | solution.py:150
  9.1 1.4 %fusion.3 = f32[128,64]{0,1:T(8,128)S(1)} fusion(f32[4096,64]{0,1:T(8,128)S(1)} %convolution_subtract_fusion, f32[4096,128]{1,0:T(8,128)S(1)} %copy-done), kind=kOutput, calls=%fused_computation.10 | convolution fusion | flops 402661376 | bytes 3178496 | tf_op jit(solution)/shard_map/dot_general | solution.py:148
  10.6 0.1 copy.27
  10.8 17.1 %all_to_all.21 = f32[32,1,896]{2,1,0:T(1,128)S(1)} all-to-all(f32[32,1,896]{2,1,0:T(1,128)S(1)} %bitcast.36), channel_id=1, replica_groups=mesh['grp'=16,'dev_0'=4,'dev_1'=4,'dev_2'=2] {'dev_0','dev_1','dev_2'}, dimensions={0} | all-to-all | bytes 229376 | tf_op jit(solution)/shard_map/all_to_all | solution.py:26
  28.0 25.2 %all_to_all.22 = f32[16,1,896]{2,1,0:T(1,128)S(1)} all-to-all(f32[16,1,896]{2,1,0:T(1,128)S(1)} %broadcast_in_dim.6), channel_id=1, replica_groups=mesh['grp'=16,'dev_0'=4,'dev_1'=4,'dev_2'=2] {'grp'}, dimensions={0} | all-to-all | bytes 114688 | tf_op jit(solution)/shard_map/all_to_all | solution.py:22
  53.3 0.7 broadcast_in_dim.7
  54.0 5.3 %all-to-all-start.2 = ((f32[32,1,896]{2,1,0:T(1,128)}), f32[32,1,896]{2,1,0:T(1,128)S(1)}, u32[]{:S(2)}, u32[]{:S(2)}) async-start(f32[32,1,896]{2,1,0:T(1,128)} %broadcast_in_dim.7), calls=%async_computation.2 | async-start | bytes 229376 | tf_op jit(solution)/shard_map/all_to_all | solution.py:22
  59.3 0.6 fusion.8
  59.9 7.0 %all-to-all-done.2 = f32[32,1,896]{2,1,0:T(1,128)S(1)} async-done(((f32[32,1,896]{2,1,0:T(1,128)}), f32[32,1,896]{2,1,0:T(1,128)S(1)}, u32[]{:S(2)}, u32[]{:S(2)}) %all-to-all-start.2) | async-done | bytes 114720 | tf_op jit(solution)/shard_map/all_to_all | solution.py:22
  66.9 0.9 %reduce.2 = f32[32,896]{1,0:T(8,128)} reduce(f32[32,1,896]{2,1,0:T(1,128)S(1)} %all-to-all-done.2, f32[]{:T(128)} %constant.12), dimensions={1}, to_apply=%all_to_all.17.reduce_sub_computation | reduce | bytes 229380 | tf_op jit(solution)/shard_map/all_to_all | solution.py:22
  67.8 1.0 %slice.16 = f32[448,64]{1,0:T(8,128)S(1)} reshape(f32[32,896]{1,0:T(8,128)} %reduce.2) | data formatting | bytes 229376 | tf_op jit(solution)/shard_map/slice | solution.py:44
  68.8 0.6 slice.23
  69.4 0.7 copy.38
  70.1 1.0 %fusion.2 = f32[128,64]{0,1:T(8,128)S(1)} fusion(f32[128,64]{0,1:T(8,128)} %copy.38, f32[224,128]{1,0:T(8,128)S(1)} %bitcast.34, f32[448,64]{1,0:T(8,128)S(1)} %slice.16), kind=kOutput, calls=%fused_computation.7 | convolution fusion | flops 12599296 | bytes 196608 | tf_op jit(solution)/shard_map/dot_general | solution.py:154
  71.2 0.3 fusion.9
  71.4 0.2 fusion.4
  71.7 3.4 %fusion = f32[4096,64]{0,1:T(8,128)} fusion(f32[4096,64]{0,1:T(8,128)S(1)} %convolution_subtract_fusion, f32[128,64]{0,1:T(8,128)S(1)} %fusion.2, f32[4096,128]{1,0:T(8,128)S(1)} %copy-done), kind=kOutput, calls=%fused_computation.2 | convolution fusion | flops 402915328 | bytes 4227072 | tf_op jit(solution)/shard_map/dot_general | solution.py:156
  75.3 0.2 convolution_add_fusion
  75.6 0.7 pad_maximum_fusion.1.augmented_ref
  76.2 8.1 %shard_map.58 = (f32[64,64]{1,0:T(8,128)}, f32[64,64]{1,0:T(8,128)}) custom-call(f32[64,128]{1,0:T(8,128)} %pad_maximum_fusion.1.augmented_ref), custom_call_target="tpu_custom_call" | custom-call | tf_op jit(solution)/shard_map/pallas_call | solution.py:131
  84.4 3.3 %fusion.12 = f32[4096,64]{0,1:T(8,128)} fusion(f32[4096,64]{0,1:T(8,128)} %fusion, f32[64,64]{1,0:T(8,128)} %get-tuple-element.5), kind=kOutput, calls=%fused_computation.24 | convolution fusion | flops 201326592 | bytes 2113536 | tf_op jit(solution)/shard_map/dot_general | solution.py:166
  (22 shorter events, 0.6 us)
Async XLA Ops:
  0.6 1.6 %copy-start = (f32[4096,128]{1,0:T(8,128)S(1)}, f32[4096,128]{1,0:T(8,128)}, u32[]{:S(2)}) copy-start(f32[4096,128]{1,0:T(8,128)} %param.3) | copy-start | bytes 6291460
  0.6 5.0 %copy-start.5 = (f32[128,64]{0,1:T(8,128)S(1)}, f32[128,64]{0,1:T(8,128)}, u32[]{:S(2)}) copy-start(f32[128,64]{0,1:T(8,128)} %param.5) | copy-start | bytes 98308
  2.2 3.5 %copy-start.1 = (f32[4096,64]{0,1:T(8,128)S(1)}, f32[4096,64]{0,1:T(8,128)}, u32[]{:S(2)}) copy-start(f32[4096,64]{0,1:T(8,128)} %param.4) | copy-start | bytes 3145732
  54.0 12.9 %all-to-all-start.2 = ((f32[32,1,896]{2,1,0:T(1,128)}), f32[32,1,896]{2,1,0:T(1,128)S(1)}, u32[]{:S(2)}, u32[]{:S(2)}) async-start(f32[32,1,896]{2,1,0:T(1,128)} %broadcast_in_dim.7), calls=%async_computation.2 | async-start | bytes 229376 | tf_op jit(solution)/shard_map/all_to_all | solution.py:22
  71.2 4.1 %copy-start.2 = (f32[128,64]{0,1:T(8,128)}, f32[128,64]{0,1:T(8,128)S(1)}, u32[]{:S(2)}) copy-start(f32[128,64]{0,1:T(8,128)S(1)} %fusion.2) | copy-start | bytes 98308
  71.7 3.4 %copy-start.4 = (f32[64,64]{1,0:T(8,128)S(1)}, f32[64,64]{1,0:T(8,128)}, u32[]{:S(2)}) copy-start(f32[64,64]{1,0:T(8,128)} %slice.23) | copy-start | bytes 49156
  71.7 3.8 %copy-start.3 = (f32[64,64]{1,0:T(8,128)S(1)}, f32[64,64]{1,0:T(8,128)}, u32[]{:S(2)}) copy-start(f32[64,64]{1,0:T(8,128)} %fusion.8) | copy-start | bytes 49156
